TPU v7x, 256 devices: a whole 4x4x8 slice. The times are simulated.
256 devices in a mesh: pair: 2 (over core), seq: 32 (over y, x, z_hi), tp: 4 (over z_lo).
Axes of the slice: x: 4, y: 4, z: 8 (z_hi: 2, z_lo: 4; z = z_hi * 4 + z_lo), core: 2. Of those that a mesh axis runs over, the one named last changes fastest.
Arguments:
- hidden: bfloat16 [36864, 3072], P(('pair', 'seq'), 'tp'), may hold values from -11 to 11
- positions: int32 [3, 36864], P(None, ('pair', 'seq')), may hold values from 0 to 63, as said below
- lengths: int32 [8], P('pair'), may hold values from 1 to 512, as said below
- step_index: int32 [1], replicated, may hold values from 0 to 7
- layer_mod: float32 [8, 3, 3072], P('pair'), may hold values from -3 to 3
- final_mod: float32 [8, 2, 3072], P('pair'), may hold values from -3 to 3
- qkv_weight: bfloat16 [3072, 3, 1536], P(None, None, 'tp'), may hold values from -0.108253175 to 0.108253175
- q_gain: float32 [128], replicated, may hold values from 0.5 to 5.5
- k_gain: float32 [128], replicated, may hold values from 0.5 to 5.5
- out_weight: bfloat16 [1536, 3072], P('tp'), may hold values from -0.15625 to 0.15625
- final_weight: bfloat16 [3072, 64], P('tp'), may hold values from -0.109375 to 0.109375
- latents: float32 [16384, 64], P(('pair', 'seq')), may hold values from -6 to 6
Outputs:
- new_hidden: bfloat16 [36864, 3072], P(('pair', 'seq'), 'tp')
- attention_lse: float32 [12, 36864], P('tp', ('pair', 'seq'))
- next_latents: float32 [16384, 64], P(('pair', 'seq'))
Inputs may be any that keep to these rules, and one draw needn't show every extreme that they name: `lengths`: some sequence has all 512 text tokens live and some sequence just one. `positions`: the first component is zero; text rows are zero; the image rows of a sequence hold each cell (row, column) of a grid 64 cells wide exactly once, the same for both sequences of a prompt.
All inputs are finite; a program needn't handle non-finite values.
Results may differ from a plain program's by a relative error of at most 0.01.
Values may be sent and summed in bfloat16 or wider, within the bound.
No kernel may reach another device: no remote copies, remote signals or barrier semaphores. Data moves between devices by JAX's collectives and lax.ppermute only.
A program may use at most 128 MiB of HBM per device.

v0:
```python
import jax
import jax.numpy as jnp
from jax import lax
from jax.sharding import PartitionSpec as P

ROPE_T = 16
ROPE_H = 56
ROPE_W = 56
STEPS = 8
IMG_DEV = 512
TXT_DEV = 64


GUIDE = 3.5
SHIFT = 3.0


def swapped(block, axis, bit):
    count = lax.axis_size(axis)
    route = []
    for low in range(count):
        high = low | 1 << bit
        if high != low and high < count:
            route += [(low, high), (high, low)]
    return lax.ppermute(block, axis, route)


def seq_route(spread, move):
    count_x = spread // 2
    route = []
    for group in range(4):
        for shard in range(spread):
            dest_x, dest_z = move(shard // 2, shard % 2, count_x)
            route.append((group * spread + shard, group * spread + (dest_x % count_x) * 2 + dest_z))
    return route


def rope_tables(ids_block):
    angle_parts = []
    for axis_pos, rope_width in ((0, ROPE_T), (1, ROPE_H), (2, ROPE_W)):
        frequencies = 10000.0 ** (-jnp.arange(0, rope_width, 2).astype(jnp.float32) / rope_width)
        angle_parts.append(ids_block[axis_pos].astype(jnp.float32)[:, None] * frequencies[None, :])
    angles = jnp.concatenate(angle_parts, axis=1)
    angles = jnp.repeat(angles, 2, axis=1)
    even = (jnp.arange(angles.shape[1]) % 2 == 0)[None, :]
    sine = jnp.sin(angles)
    return (jnp.cos(angles), jnp.where(even, -sine, sine), even)


def rotate(tensor, cosine, signed_sine, even):
    partner = jnp.where(
        even[None], jnp.roll(tensor, -1, axis=-1), jnp.roll(tensor, 1, axis=-1)
    )
    return tensor * cosine[None] + partner * signed_sine[None]


def rms_gain(tensor, gain_vec):
    return tensor * lax.rsqrt(jnp.mean(tensor * tensor, axis=-1, keepdims=True) + 1e-06) * gain_vec


def modulate(features, shift_vec, scale_vec):
    row_mean = jnp.mean(features, axis=-1, keepdims=True)
    row_var = jnp.mean(features * features, axis=-1, keepdims=True) - row_mean * row_mean
    return (features - row_mean) * lax.rsqrt(row_var + 1e-06) * (1.0 + scale_vec) + shift_vec


def sigma_at(step_now):
    time_now = 1.0 - step_now.astype(jnp.float32) / STEPS
    return SHIFT * time_now / (1.0 + (SHIFT - 1.0) * time_now)


def fold_block(state, queries, key_block, value_block, shard, text_count):
    row_max, row_sum, weighted = state
    rows_dev = key_block.shape[1]
    offset = jnp.arange(rows_dev, dtype=jnp.int32)
    text_index = shard * TXT_DEV + offset - IMG_DEV
    is_live = (offset < IMG_DEV) | (text_index < text_count)
    score_scale = queries.shape[-1] ** (-0.5)
    scores = (
        jnp.einsum("hqd,hkd->hqk", queries, key_block, preferred_element_type=jnp.float32)
        * score_scale
    )
    scores = jnp.where(is_live[None, None, :], scores, -jnp.inf)
    new_max = jnp.maximum(row_max, jnp.max(scores, axis=2))
    exps = jnp.exp(scores - new_max[:, :, None])
    decay = jnp.exp(row_max - new_max)
    row_sum = row_sum * decay + jnp.sum(exps, axis=2)
    weighted = weighted * decay[:, :, None] + jnp.einsum(
        "hqk,hkd->hqd", exps.astype(jnp.bfloat16), value_block, preferred_element_type=jnp.float32
    )
    return (new_max, row_sum, weighted)


def merge_states(first, second):
    max_a, sum_a, acc_a = first
    max_b, sum_b, acc_b = second
    new_max = jnp.maximum(max_a, max_b)
    scale_a = jnp.exp(max_a - new_max)
    scale_b = jnp.exp(max_b - new_max)
    return (
        new_max,
        sum_a * scale_a + sum_b * scale_b,
        acc_a * scale_a[:, :, None] + acc_b * scale_b[:, :, None],
    )


def tp_sum(tree):
    count = lax.axis_size("tp")
    bit = 0
    while 1 << bit < count:
        far = swapped(tree, "tp", bit)
        tree = jax.tree.map(lambda a, b: a + b, tree, far)
        bit += 1
    return tree


def on_device(
    hidden,
    positions,
    lengths,
    step_index,
    layer_mod,
    final_mod,
    qkv_weight,
    q_gain,
    k_gain,
    out_weight,
    final_weight,
    latents,
):
    spread = lax.axis_size("seq") // 4
    bit_count = spread.bit_length() - 1
    seq_pos = lax.axis_index("seq")
    local_seq = seq_pos // spread
    shard_pos = seq_pos % spread
    count_x = spread // 2
    my_x = shard_pos // 2
    my_z = shard_pos % 2
    tp_pos = lax.axis_index("tp")
    local_width = hidden.shape[1]
    tp_count = lax.axis_size("tp")
    parts = [hidden]
    for shift in range(1, tp_count):
        route = [(src, (src + shift) % tp_count) for src in range(tp_count)]
        parts.append(lax.ppermute(hidden, "tp", route))
    stacked = jnp.stack(parts)
    gathered = jnp.concatenate(
        [
            lax.dynamic_index_in_dim(stacked, (tp_pos - owner) % tp_count, 0, keepdims=False)
            for owner in range(tp_count)
        ],
        axis=1,
    )
    model_width = gathered.shape[1]
    rows_dev = gathered.shape[0]
    layer_terms = lax.dynamic_index_in_dim(layer_mod, local_seq, 0, keepdims=False)
    text_count = lax.dynamic_index_in_dim(lengths, local_seq, 0, keepdims=False)
    modulated = modulate(gathered.astype(jnp.float32), layer_terms[0], layer_terms[1]).astype(
        jnp.bfloat16
    )
    head_dim = q_gain.shape[0]
    head_cols = qkv_weight.shape[2]
    heads_here = head_cols // head_dim
    weight4 = qkv_weight.reshape(model_width, 3, heads_here, head_dim)
    projected = jnp.einsum(
        "rf,fchd->chrd", modulated, weight4, preferred_element_type=jnp.float32
    )
    cosine, signed_sine, even = rope_tables(positions)
    queries = rotate(rms_gain(projected[0], q_gain), cosine, signed_sine, even).astype(jnp.bfloat16)
    key_rot = rotate(rms_gain(projected[1], k_gain), cosine, signed_sine, even).astype(jnp.bfloat16)
    values = projected[2].astype(jnp.bfloat16)
    own = jnp.stack([key_rot, values])

    to_left = seq_route(spread, lambda x, z, n: (x - 1, z))
    to_right = seq_route(spread, lambda x, z, n: (x + 1, z))
    to_other_z = seq_route(spread, lambda x, z, n: (x, 1 - z))

    def shard_of(x, z):
        return (x % count_x) * 2 + z

    got_z = lax.ppermute(own, "seq", to_other_z)
    got_right = lax.ppermute(own, "seq", to_left)
    got_left = lax.ppermute(own, "seq", to_right)

    softmax_state = (
        jnp.full((heads_here, rows_dev), -jnp.inf, jnp.float32),
        jnp.zeros((heads_here, rows_dev), jnp.float32),
        jnp.zeros((heads_here, rows_dev, head_dim), jnp.float32),
    )
    softmax_state = fold_block(softmax_state, queries, own[0], own[1], shard_pos, text_count)

    z_from_right, far_keys = lax.ppermute((got_z, got_right[0]), "seq", to_left)
    z_from_left, far_values = lax.ppermute((got_z, got_left[1]), "seq", to_right)

    other_z = 1 - my_z
    softmax_state = fold_block(
        softmax_state, queries, got_z[0], got_z[1], shard_of(my_x, other_z), text_count
    )
    softmax_state = fold_block(
        softmax_state, queries, got_right[0], got_right[1], shard_of(my_x + 1, my_z), text_count
    )
    softmax_state = fold_block(
        softmax_state, queries, got_left[0], got_left[1], shard_of(my_x - 1, my_z), text_count
    )

    far_z_keys = lax.ppermute(z_from_right[0], "seq", to_left)
    far_z_values = lax.ppermute(z_from_left[1], "seq", to_right)

    late_state = (
        jnp.full((heads_here, rows_dev), -jnp.inf, jnp.float32),
        jnp.zeros((heads_here, rows_dev), jnp.float32),
        jnp.zeros((heads_here, rows_dev, head_dim), jnp.float32),
    )
    late_state = fold_block(
        late_state, queries, far_keys, far_values, shard_of(my_x + 2, my_z), text_count
    )
    late_state = fold_block(
        late_state, queries, z_from_right[0], z_from_right[1], shard_of(my_x + 1, other_z), text_count
    )
    late_state = fold_block(
        late_state, queries, z_from_left[0], z_from_left[1], shard_of(my_x - 1, other_z), text_count
    )
    softmax_state = fold_block(
        softmax_state, queries, far_z_keys, far_z_values, shard_of(my_x + 2, other_z), text_count
    )
    softmax_state = merge_states(softmax_state, late_state)

    row_max, row_sum, weighted = softmax_state
    attended = (weighted / row_sum[:, :, None]).astype(jnp.bfloat16)
    log_sums = row_max + jnp.log(row_sum)
    hold = jnp.minimum(jnp.abs(queries[0, 0, 0]), 0).astype(out_weight.dtype)
    attended_parts = [attended]
    weight_parts = [lax.dynamic_slice_in_dim(out_weight, tp_pos * local_width, local_width, 1)]
    for shift in range(1, tp_count):
        route = [(src, (src + shift) % tp_count) for src in range(tp_count)]
        dest = (tp_pos + shift) % tp_count
        weight_send = lax.dynamic_slice_in_dim(out_weight, dest * local_width, local_width, 1)
        weight_parts.append(lax.ppermute(weight_send + hold, "tp", route))
        attended_parts.append(lax.ppermute(attended, "tp", route))
    all_attended = jnp.stack(attended_parts)
    all_weights = jnp.stack(weight_parts).reshape(tp_count, heads_here, head_dim, local_width)
    update = jnp.einsum(
        "khrd,khdf->rf", all_attended, all_weights, preferred_element_type=jnp.float32
    )
    gate_slice = lax.dynamic_slice_in_dim(layer_terms[2], tp_pos * local_width, local_width, 0)
    new_hidden = (hidden.astype(jnp.float32) + gate_slice * update).astype(jnp.bfloat16)

    final_terms = lax.dynamic_index_in_dim(final_mod, local_seq, 0, keepdims=False)
    final_shift = lax.dynamic_slice_in_dim(final_terms[0], tp_pos * local_width, local_width, 0)
    final_scale = lax.dynamic_slice_in_dim(final_terms[1], tp_pos * local_width, local_width, 0)
    image_rows = new_hidden[:IMG_DEV].astype(jnp.float32)
    weight = final_weight.astype(jnp.float32)
    scale_one = 1.0 + final_scale
    highest = lax.Precision.HIGHEST
    terms = (
        jnp.sum(image_rows, axis=1),
        jnp.sum(image_rows * image_rows, axis=1),
        jnp.dot(image_rows * scale_one, weight, precision=highest),
        jnp.dot(scale_one[None, :], weight, precision=highest),
        jnp.dot(final_shift[None, :], weight, precision=highest),
    )
    row_sums, squares, scaled_proj, scale_proj, shift_proj = tp_sum(terms)
    row_mean = row_sums / model_width
    inv_std = lax.rsqrt(squares / model_width - row_mean * row_mean + 1e-06)
    velocity = (
        inv_std[:, None] * (scaled_proj - row_mean[:, None] * scale_proj) + shift_proj
    )

    half_rows = IMG_DEV // 2
    is_cond = local_seq % 2 == 0
    outgoing = jnp.where(is_cond, velocity[half_rows:], velocity[:half_rows])
    partner_half = swapped(outgoing, "seq", bit_count)
    own_half = jnp.where(is_cond, velocity[:half_rows], velocity[half_rows:])
    cond_vel = jnp.where(is_cond, own_half, partner_half)
    uncond_vel = jnp.where(is_cond, partner_half, own_half)
    guided = uncond_vel + GUIDE * (cond_vel - uncond_vel)
    step_now = step_index[0]
    time_step = sigma_at(step_now + 1) - sigma_at(step_now)
    return (new_hidden, log_sums, latents + time_step * guided)


def solution(mesh):
    return jax.shard_map(
        on_device,
        mesh=mesh,
        in_specs=(
            P(("pair", "seq"), "tp"),
            P(None, ("pair", "seq")),
            P("pair"),
            P(),
            P("pair", None, None),
            P("pair", None, None),
            P(None, None, "tp"),
            P(),
            P(),
            P("tp", None),
            P("tp", None),
            P(("pair", "seq"), None),
        ),
        out_specs=(P(("pair", "seq"), "tp"), P("tp", ("pair", "seq")), P(("pair", "seq"), None)),
        check_vma=False,
    )
```

profile of v0, /device:TPU:40, one launch (start us, length us, event | category | flops | bytes accessed | tf_op | source)
XLA Modules:
  0.0 276.1 jit_solution(8182691514567162998)
XLA Ops:
  13.5 10.4 %copy.27 = bf16[3072,3,384]{0,2,1:T(8,128)(2,1)} copy(bf16[3072,3,384]{2,0,1:T(8,128)(2,1)} %param.18) | data formatting | bytes 14155776 | tf_op args[6]
  28.0 32.2 %collective-permute-done.24 = f32[1,64]{1,0:T(1,128)S(1)} collective-permute-done((f32[1,64]{1,0:T(1,128)S(1)}, f32[1,64]{1,0:T(1,128)S(1)}, u32[]{:S(2)}, u32[]{:S(2)}) %collective-permute-start.24) | collective-permute-done | bytes 288 | tf_op jit(solution)/shard_map/ppermute | solution.py:25
  61.7 17.0 %collective-permute-done.1 = bf16[576,768]{1,0:T(8,128)(2,1)} collective-permute-done((bf16[576,768]{1,0:T(8,128)(2,1)}, bf16[576,768]{1,0:T(8,128)(2,1)}, u32[]{:S(2)}, u32[]{:S(2)}) %collective-permute-start.1) | collective-permute-done | bytes 884768 | tf_op jit(solution)/shard_map/ppermute | solution.py:145
  83.0 3.3 %convert_reduce_fusion = (f32[576]{0:T(1024)S(1)}, f32[576]{0:T(1024)S(1)}) fusion(bf16[576,768]{1,0:T(8,128)(2,1)S(1)} %get-tuple-element.32, bf16[576,768]{1,0:T(8,128)(2,1)S(1)} %get-tuple-element.33, bf16[576,768]{1,0:T(8,128)(2,1)S(1)} %get-tuple-element.34, bf16[576,768]{1,0:T(8,128)(2,1)S(1)} %get-tuple-element.31), kind=kLoop, calls=%fused_computation.2 | loop fusion | flops 19463040 | bytes 3543552 | tf_op jit(solution)/shard_map/reduce_sum | solution.py:62
  86.4 5.2 %fusion.71 = f32[3,3,576,128]{3,2,1,0:T(8,128)S(1)} fusion(bf16[3072,3,3,128]{0,3,2,1:T(8,128)(2,1)S(1)} %bitcast.141, f32[3072]{0:T(1024)S(1)} %bitcast.146, f32[3072]{0:T(1024)S(1)} %bitcast.145, f32[576]{0:T(1024)S(1)} %get-tuple-element.60, f32[576]{0:T(1024)S(1)} %get-tuple-element.59, bf16[576,768]{1,0:T(8,128)(2,1)S(1)} %get-tuple-element.32, ...), kind=kOutput, calls=%fused_computation.88 | convolution fusion | flops 4099866624 | bytes 13300224 | tf_op jit(solution)/shard_map/rf,fchd->chrd/dot_general | solution.py:165
  95.1 22.3 %collective-permute-start.3 = (bf16[2,3,576,128]{3,2,1,0:T(8,128)(2,1)S(1)}, bf16[2,3,576,128]{3,2,1,0:T(8,128)(2,1)S(1)}, u32[]{:S(2)}, u32[]{:S(2)}) collective-permute-start(bf16[2,3,576,128]{3,2,1,0:T(8,128)(2,1)S(1)} %pad_maximum_fusion.3), channel_id=1, source_target_pairs={{0,4},{4,0},{8,12},{12,8},{16,20},{20,16},{24,28},{28,24},{32,36},... | collective-permute-start | bytes 2654216 | tf_op jit(solution)/shard_map/ppermute | solution.py:181
  117.4 2.8 collective-permute-start.4
  126.3 5.5 %collective-permute-done.4 = bf16[2,3,576,128]{3,2,1,0:T(8,128)(2,1)S(1)} collective-permute-done((bf16[2,3,576,128]{3,2,1,0:T(8,128)(2,1)S(1)}, bf16[2,3,576,128]{3,2,1,0:T(8,128)(2,1)S(1)}, u32[]{:S(2)}, u32[]{:S(2)}) %collective-permute-start.4) | collective-permute-done | bytes 884768 | tf_op jit(solution)/shard_map/ppermute | solution.py:182
  132.7 6.7 %collective-permute-done.3 = bf16[2,3,576,128]{3,2,1,0:T(8,128)(2,1)S(1)} collective-permute-done((bf16[2,3,576,128]{3,2,1,0:T(8,128)(2,1)S(1)}, bf16[2,3,576,128]{3,2,1,0:T(8,128)(2,1)S(1)}, u32[]{:S(2)}, u32[]{:S(2)}) %collective-permute-start.3) | collective-permute-done | bytes 884768 | tf_op jit(solution)/shard_map/ppermute | solution.py:181
  140.2 8.7 %collective-permute-start.6 = (bf16[2,3,576,128]{3,2,1,0:T(8,128)(2,1)S(1)}, bf16[2,3,576,128]{3,2,1,0:T(8,128)(2,1)S(1)}, u32[]{:S(2)}, u32[]{:S(2)}) collective-permute-start(bf16[2,3,576,128]{3,2,1,0:T(8,128)(2,1)S(1)} %collective-permute-done.3), channel_id=1, source_target_pairs={{0,24},{4,28},{8,0},{12,4},{16,8},{20,12},{24,16},{28,20},{32,56},... | collective-permute-start | bytes 2654216 | tf_op jit(solution)/shard_map/ppermute | solution.py:192
  150.6 4.7 %collective-permute-done.10 = bf16[3,576,128]{2,1,0:T(8,128)(2,1)S(1)} collective-permute-done((bf16[3,576,128]{2,1,0:T(8,128)(2,1)S(1)}, bf16[3,576,128]{2,1,0:T(8,128)(2,1)S(1)}, u32[]{:S(2)}, u32[]{:S(2)}) %collective-permute-start.10) | collective-permute-done | bytes 442400 | tf_op jit(solution)/shard_map/ppermute | solution.py:192
  158.9 10.7 %collective-permute-done.6 = bf16[2,3,576,128]{3,2,1,0:T(8,128)(2,1)S(1)} collective-permute-done((bf16[2,3,576,128]{3,2,1,0:T(8,128)(2,1)S(1)}, bf16[2,3,576,128]{3,2,1,0:T(8,128)(2,1)S(1)}, u32[]{:S(2)}, u32[]{:S(2)}) %collective-permute-start.6) | collective-permute-done | bytes 884768 | tf_op jit(solution)/shard_map/ppermute | solution.py:192
  169.5 3.4 %collective-permute-start.16 = (bf16[384,768]{1,0:T(8,128)(2,1)}, bf16[384,768]{1,0:T(8,128)(2,1)}, u32[]{:S(2)}, u32[]{:S(2)}) collective-permute-start(bf16[384,768]{1,0:T(8,128)(2,1)} %get-tuple-element.40), channel_id=1, source_target_pairs={{0,2},{1,3},{2,0},{3,1},{4,6},{5,7},{6,4},{7,5},{8,10},{9,11},{10,... | collective-permute-start | bytes 1769480 | tf_op jit(solution)/shard_map/ppermute | solution.py:238
  173.8 3.9 %collective-permute-start.7 = (bf16[3,576,128]{2,1,0:T(8,128)(2,1)S(1)}, bf16[3,576,128]{2,1,0:T(8,128)(2,1)S(1)}, u32[]{:S(2)}, u32[]{:S(2)}) collective-permute-start(bf16[3,576,128]{2,1,0:T(8,128)(2,1)S(1)} %slice_bitcast_fusion.6), channel_id=1, source_target_pairs={{0,24},{4,28},{8,0},{12,4},{16,8},{20,12},{24,16},{28,20},{32,56},... | collective-permute-start | bytes 1327112 | tf_op jit(solution)/shard_map/ppermute | solution.py:206
  178.6 5.0 %collective-permute-done.7 = bf16[3,576,128]{2,1,0:T(8,128)(2,1)S(1)} collective-permute-done((bf16[3,576,128]{2,1,0:T(8,128)(2,1)S(1)}, bf16[3,576,128]{2,1,0:T(8,128)(2,1)S(1)}, u32[]{:S(2)}, u32[]{:S(2)}) %collective-permute-start.7) | collective-permute-done | bytes 442400 | tf_op jit(solution)/shard_map/ppermute | solution.py:206
  200.1 2.8 %fusion.119 = f32[3,576,128]{2,1,0:T(8,128)S(1)} fusion(f32[3,576,576]{1,2,0:T(8,128)S(1)} %get-tuple-element.76, f32[3,576]{1,0:T(4,128)S(1)} %get-tuple-element.75, pred[576]{0:T(1024)(128)(4,1)S(1)} %get-tuple-element.88, f32[3,576]{1,0:T(4,128)S(1)} %get-tuple-element.23, f32[3,576]{1,0:T(4,128)S(1)} %get-tuple-element.58, f32[3,3,576,128]{3,2,1,0:T(8,128)} %copy-done.1), kind=kOutput, calls=%fused_computation.104 | convolution fusion | flops 259227648 | bytes 5329728 | tf_op jit(solution)/shard_map/hqk,hkd->hqd/dot_general | solution.py:88
  203.0 3.3 %collective-permute-done.11 = bf16[3,576,128]{2,1,0:T(8,128)(2,1)S(1)} collective-permute-done((bf16[3,576,128]{2,1,0:T(8,128)(2,1)}, bf16[3,576,128]{2,1,0:T(8,128)(2,1)S(1)}, u32[]{:S(2)}, u32[]{:S(2)}) %collective-permute-start.11) | collective-permute-done | bytes 442400 | tf_op jit(solution)/shard_map/ppermute | solution.py:193
  220.2 20.7 %collective-permute-done.17 = bf16[384,768]{1,0:T(8,128)(2,1)} collective-permute-done((bf16[384,768]{1,0:T(8,128)(2,1)S(1)}, bf16[384,768]{1,0:T(8,128)(2,1)}, u32[]{:S(2)}, u32[]{:S(2)}) %collective-permute-start.17) | collective-permute-done | bytes 589856 | tf_op jit(solution)/shard_map/ppermute | solution.py:238
  240.9 4.1 %collective-permute-done.12 = bf16[3,576,128]{2,1,0:T(8,128)(2,1)S(1)} collective-permute-done((bf16[3,576,128]{2,1,0:T(8,128)(2,1)}, bf16[3,576,128]{2,1,0:T(8,128)(2,1)S(1)}, u32[]{:S(2)}, u32[]{:S(2)}) %collective-permute-start.12) | collective-permute-done | bytes 442400 | tf_op jit(solution)/shard_map/ppermute | solution.py:239
  245.1 4.7 %collective-permute-done.13 = bf16[3,576,128]{2,1,0:T(8,128)(2,1)} collective-permute-done((bf16[3,576,128]{2,1,0:T(8,128)(2,1)}, bf16[3,576,128]{2,1,0:T(8,128)(2,1)}, u32[]{:S(2)}, u32[]{:S(2)}) %collective-permute-start.13) | collective-permute-done | bytes 442400 | tf_op jit(solution)/shard_map/ppermute | solution.py:239
  249.8 2.8 %collective-permute-done.14 = bf16[3,576,128]{2,1,0:T(8,128)(2,1)} collective-permute-done((bf16[3,576,128]{2,1,0:T(8,128)(2,1)}, bf16[3,576,128]{2,1,0:T(8,128)(2,1)}, u32[]{:S(2)}, u32[]{:S(2)}) %collective-permute-start.14) | collective-permute-done | bytes 442400 | tf_op jit(solution)/shard_map/ppermute | solution.py:239
  252.6 3.4 %fusion.69 = bf16[576,768]{1,0:T(8,128)(2,1)S(1)} fusion(bf16[576,768]{1,0:T(8,128)(2,1)S(1)} %copy-done.3, bf16[1,3,128,768]{3,2,0,1:T(8,128)(2,1)} %bitcast.40, bf16[1,3,128,768]{3,2,0,1:T(8,128)(2,1)} %bitcast.39, bf16[1,3,128,768]{3,2,0,1:T(8,128)(2,1)} %bitcast.38, bf16[1,3,128,768]{3,2,0,1:T(8,128)(2,1)S(1)} %bitcast.144, ...), kind=kOutput, calls=%fused_computation.86 | convolution fusion | flops 1366917120 | bytes 5901312 | tf_op jit(solution)/shard_map/khrd,khdf->rf/dot_general | solution.py:242
  265.6 5.0 %collective-permute-done.23 = f32[512,64]{0,1:T(8,128)S(1)} collective-permute-done((f32[512,64]{0,1:T(8,128)S(1)}, f32[512,64]{0,1:T(8,128)S(1)}, u32[]{:S(2)}, u32[]{:S(2)}) %collective-permute-start.23) | collective-permute-done | bytes 131104 | tf_op jit(solution)/shard_map/ppermute | solution.py:25
  271.9 3.1 %collective-permute-done.28 = f32[256,64]{0,1:T(8,128)S(1)} collective-permute-done((f32[256,64]{0,1:T(8,128)S(1)}, f32[256,64]{0,1:T(8,128)S(1)}, u32[]{:S(2)}, u32[]{:S(2)}) %collective-permute-start.28) | collective-permute-done | bytes 65568 | tf_op jit(solution)/shard_map/ppermute | solution.py:25
  (158 shorter events, 80.9 us)
Async XLA Ops:
  0.6 61.1 %collective-permute-start = (bf16[576,768]{1,0:T(8,128)(2,1)}, bf16[576,768]{1,0:T(8,128)(2,1)S(1)}, u32[]{:S(2)}, u32[]{:S(2)}) collective-permute-start(bf16[576,768]{1,0:T(8,128)(2,1)} %param.12), channel_id=1, source_target_pairs={{0,1},{1,2},{2,3},{3,0},{4,5},{5,6},{6,7},{7,4},{8,9},{9,10},{10,1... | collective-permute-start | bytes 2654216 | tf_op jit(solution)/shard_map/ppermute | solution.py:145
  2.6 76.1 %collective-permute-start.1 = (bf16[576,768]{1,0:T(8,128)(2,1)}, bf16[576,768]{1,0:T(8,128)(2,1)}, u32[]{:S(2)}, u32[]{:S(2)}) collective-permute-start(bf16[576,768]{1,0:T(8,128)(2,1)} %param.12), channel_id=1, source_target_pairs={{0,2},{1,3},{2,0},{3,1},{4,6},{5,7},{6,4},{7,5},{8,10},{9,11},{10,... | collective-permute-start | bytes 2654216 | tf_op jit(solution)/shard_map/ppermute | solution.py:145
  4.1 76.8 %collective-permute-start.2 = (bf16[576,768]{1,0:T(8,128)(2,1)}, bf16[576,768]{1,0:T(8,128)(2,1)}, u32[]{:S(2)}, u32[]{:S(2)}) collective-permute-start(bf16[576,768]{1,0:T(8,128)(2,1)} %param.12), channel_id=1, source_target_pairs={{0,3},{1,0},{2,1},{3,2},{4,7},{5,4},{6,5},{7,6},{8,11},{9,8},{10,9... | collective-permute-start | bytes 2654216 | tf_op jit(solution)/shard_map/ppermute | solution.py:145
  6.9 53.4 %collective-permute-start.24 = (f32[1,64]{1,0:T(1,128)S(1)}, f32[1,64]{1,0:T(1,128)S(1)}, u32[]{:S(2)}, u32[]{:S(2)}) collective-permute-start(f32[1,64]{1,0:T(1,128)S(1)} %fusion.170), channel_id=1, source_target_pairs={{0,1},{1,0},{2,3},{3,2},{4,5},{5,4},{6,7},{7,6},{8,9},{9,8},{10,11... | collective-permute-start | bytes 776 | tf_op jit(solution)/shard_map/ppermute | solution.py:25
  8.8 204.1 %collective-permute-start.26 = (f32[1,64]{1,0:T(1,128)S(1)}, f32[1,64]{1,0:T(1,128)S(1)}, u32[]{:S(2)}, u32[]{:S(2)}) collective-permute-start(f32[1,64]{1,0:T(1,128)S(1)} %fusion.169), channel_id=1, source_target_pairs={{0,1},{1,0},{2,3},{3,2},{4,5},{5,4},{6,7},{7,6},{8,9},{9,8},{10,11... | collective-permute-start | bytes 776 | tf_op jit(solution)/shard_map/ppermute | solution.py:25
  60.3 154.6 %collective-permute-start.25 = (f32[1,64]{1,0:T(1,128)S(1)}, f32[1,64]{1,0:T(1,128)S(1)}, u32[]{:S(2)}, u32[]{:S(2)}) collective-permute-start(f32[1,64]{1,0:T(1,128)S(1)} %add.614), channel_id=1, source_target_pairs={{0,2},{2,0},{1,3},{3,1},{4,6},{6,4},{5,7},{7,5},{8,10},{10,8},{9,1... | collective-permute-start | bytes 776 | tf_op jit(solution)/shard_map/ppermute | solution.py:25
  95.1 44.3 %collective-permute-start.3 = (bf16[2,3,576,128]{3,2,1,0:T(8,128)(2,1)S(1)}, bf16[2,3,576,128]{3,2,1,0:T(8,128)(2,1)S(1)}, u32[]{:S(2)}, u32[]{:S(2)}) collective-permute-start(bf16[2,3,576,128]{3,2,1,0:T(8,128)(2,1)S(1)} %pad_maximum_fusion.3), channel_id=1, source_target_pairs={{0,4},{4,0},{8,12},{12,8},{16,20},{20,16},{24,28},{28,24},{32,36},... | collective-permute-start | bytes 2654216 | tf_op jit(solution)/shard_map/ppermute | solution.py:181
  117.4 14.4 %collective-permute-start.4 = (bf16[2,3,576,128]{3,2,1,0:T(8,128)(2,1)S(1)}, bf16[2,3,576,128]{3,2,1,0:T(8,128)(2,1)S(1)}, u32[]{:S(2)}, u32[]{:S(2)}) collective-permute-start(bf16[2,3,576,128]{3,2,1,0:T(8,128)(2,1)S(1)} %pad_maximum_fusion.3), channel_id=1, source_target_pairs={{0,24},{4,28},{8,0},{12,4},{16,8},{20,12},{24,16},{28,20},{32,56},... | collective-permute-start | bytes 2654216 | tf_op jit(solution)/shard_map/ppermute | solution.py:182
  120.2 20.0 %collective-permute-start.5 = (bf16[2,3,576,128]{3,2,1,0:T(8,128)(2,1)S(1)}, bf16[2,3,576,128]{3,2,1,0:T(8,128)(2,1)S(1)}, u32[]{:S(2)}, u32[]{:S(2)}) collective-permute-start(bf16[2,3,576,128]{3,2,1,0:T(8,128)(2,1)S(1)} %pad_maximum_fusion.3), channel_id=1, source_target_pairs={{0,8},{4,12},{8,16},{12,20},{16,24},{20,28},{24,0},{28,4},{32,40},... | collective-permute-start | bytes 2654216 | tf_op jit(solution)/shard_map/ppermute | solution.py:183
  131.8 85.8 %collective-permute-start.15 = (bf16[384,768]{1,0:T(8,128)(2,1)}, bf16[384,768]{1,0:T(8,128)(2,1)}, u32[]{:S(2)}, u32[]{:S(2)}) collective-permute-start(bf16[384,768]{1,0:T(8,128)(2,1)} %get-tuple-element.38), channel_id=1, source_target_pairs={{0,1},{1,2},{2,3},{3,0},{4,5},{5,6},{6,7},{7,4},{8,9},{9,10},{10,1... | collective-permute-start | bytes 1769480 | tf_op jit(solution)/shard_map/ppermute | solution.py:238
  139.4 15.9 %collective-permute-start.10 = (bf16[3,576,128]{2,1,0:T(8,128)(2,1)S(1)}, bf16[3,576,128]{2,1,0:T(8,128)(2,1)S(1)}, u32[]{:S(2)}, u32[]{:S(2)}) collective-permute-start(bf16[3,576,128]{2,1,0:T(8,128)(2,1)S(1)} %slice_bitcast_fusion.12), channel_id=1, source_target_pairs={{0,24},{4,28},{8,0},{12,4},{16,8},{20,12},{24,16},{28,20},{32,56},... | collective-permute-start | bytes 1327112 | tf_op jit(solution)/shard_map/ppermute | solution.py:192
  140.2 29.3 %collective-permute-start.6 = (bf16[2,3,576,128]{3,2,1,0:T(8,128)(2,1)S(1)}, bf16[2,3,576,128]{3,2,1,0:T(8,128)(2,1)S(1)}, u32[]{:S(2)}, u32[]{:S(2)}) collective-permute-start(bf16[2,3,576,128]{3,2,1,0:T(8,128)(2,1)S(1)} %collective-permute-done.3), channel_id=1, source_target_pairs={{0,24},{4,28},{8,0},{12,4},{16,8},{20,12},{24,16},{28,20},{32,56},... | collective-permute-start | bytes 2654216 | tf_op jit(solution)/shard_map/ppermute | solution.py:192
  155.3 18.4 %collective-permute-start.8 = (bf16[2,3,576,128]{3,2,1,0:T(8,128)(2,1)S(1)}, bf16[2,3,576,128]{3,2,1,0:T(8,128)(2,1)S(1)}, u32[]{:S(2)}, u32[]{:S(2)}) collective-permute-start(bf16[2,3,576,128]{3,2,1,0:T(8,128)(2,1)S(1)} %collective-permute-done.3), channel_id=1, source_target_pairs={{0,8},{4,12},{8,16},{12,20},{16,24},{20,28},{24,0},{28,4},{32,40},... | collective-permute-start | bytes 2654216 | tf_op jit(solution)/shard_map/ppermute | solution.py:193
  169.5 49.7 %collective-permute-start.16 = (bf16[384,768]{1,0:T(8,128)(2,1)}, bf16[384,768]{1,0:T(8,128)(2,1)}, u32[]{:S(2)}, u32[]{:S(2)}) collective-permute-start(bf16[384,768]{1,0:T(8,128)(2,1)} %get-tuple-element.40), channel_id=1, source_target_pairs={{0,2},{1,3},{2,0},{3,1},{4,6},{5,7},{6,4},{7,5},{8,10},{9,11},{10,... | collective-permute-start | bytes 1769480 | tf_op jit(solution)/shard_map/ppermute | solution.py:238
  173.8 9.8 %collective-permute-start.7 = (bf16[3,576,128]{2,1,0:T(8,128)(2,1)S(1)}, bf16[3,576,128]{2,1,0:T(8,128)(2,1)S(1)}, u32[]{:S(2)}, u32[]{:S(2)}) collective-permute-start(bf16[3,576,128]{2,1,0:T(8,128)(2,1)S(1)} %slice_bitcast_fusion.6), channel_id=1, source_target_pairs={{0,24},{4,28},{8,0},{12,4},{16,8},{20,12},{24,16},{28,20},{32,56},... | collective-permute-start | bytes 1327112 | tf_op jit(solution)/shard_map/ppermute | solution.py:206
  183.5 12.2 %collective-permute-start.9 = (bf16[3,576,128]{2,1,0:T(8,128)(2,1)S(1)}, bf16[3,576,128]{2,1,0:T(8,128)(2,1)S(1)}, u32[]{:S(2)}, u32[]{:S(2)}) collective-permute-start(bf16[3,576,128]{2,1,0:T(8,128)(2,1)S(1)} %slice_bitcast_fusion.5), channel_id=1, source_target_pairs={{0,8},{4,12},{8,16},{12,20},{16,24},{20,28},{24,0},{28,4},{32,40},... | collective-permute-start | bytes 1327112 | tf_op jit(solution)/shard_map/ppermute | solution.py:207
  195.8 10.5 %collective-permute-start.11 = (bf16[3,576,128]{2,1,0:T(8,128)(2,1)}, bf16[3,576,128]{2,1,0:T(8,128)(2,1)S(1)}, u32[]{:S(2)}, u32[]{:S(2)}) collective-permute-start(bf16[3,576,128]{2,1,0:T(8,128)(2,1)} %slice_bitcast_fusion.7), channel_id=1, source_target_pairs={{0,8},{4,12},{8,16},{12,20},{16,24},{20,28},{24,0},{28,4},{32,40},... | collective-permute-start | bytes 1327112 | tf_op jit(solution)/shard_map/ppermute | solution.py:193
  206.3 34.7 %collective-permute-start.17 = (bf16[384,768]{1,0:T(8,128)(2,1)S(1)}, bf16[384,768]{1,0:T(8,128)(2,1)}, u32[]{:S(2)}, u32[]{:S(2)}) collective-permute-start(bf16[384,768]{1,0:T(8,128)(2,1)S(1)} %copy-done.11), channel_id=1, source_target_pairs={{0,3},{1,0},{2,1},{3,2},{4,7},{5,4},{6,5},{7,6},{8,11},{9,8},{10,9... | collective-permute-start | bytes 1769480 | tf_op jit(solution)/shard_map/ppermute | solution.py:238
  212.9 32.2 %collective-permute-start.12 = (bf16[3,576,128]{2,1,0:T(8,128)(2,1)}, bf16[3,576,128]{2,1,0:T(8,128)(2,1)S(1)}, u32[]{:S(2)}, u32[]{:S(2)}) collective-permute-start(bf16[3,576,128]{2,1,0:T(8,128)(2,1)} %fusion.134), channel_id=1, source_target_pairs={{0,1},{1,2},{2,3},{3,0},{4,5},{5,6},{6,7},{7,4},{8,9},{9,10},{10,1... | collective-permute-start | bytes 1327112 | tf_op jit(solution)/shard_map/ppermute | solution.py:239
  214.9 34.9 %collective-permute-start.13 = (bf16[3,576,128]{2,1,0:T(8,128)(2,1)}, bf16[3,576,128]{2,1,0:T(8,128)(2,1)}, u32[]{:S(2)}, u32[]{:S(2)}) collective-permute-start(bf16[3,576,128]{2,1,0:T(8,128)(2,1)} %fusion.134), channel_id=1, source_target_pairs={{0,2},{1,3},{2,0},{3,1},{4,6},{5,7},{6,4},{7,5},{8,10},{9,11},{10,... | collective-permute-start | bytes 1327112 | tf_op jit(solution)/shard_map/ppermute | solution.py:239
  217.6 35.0 %collective-permute-start.14 = (bf16[3,576,128]{2,1,0:T(8,128)(2,1)}, bf16[3,576,128]{2,1,0:T(8,128)(2,1)}, u32[]{:S(2)}, u32[]{:S(2)}) collective-permute-start(bf16[3,576,128]{2,1,0:T(8,128)(2,1)} %fusion.134), channel_id=1, source_target_pairs={{0,3},{1,0},{2,1},{3,2},{4,7},{5,4},{6,5},{7,6},{8,11},{9,8},{10,9... | collective-permute-start | bytes 1327112 | tf_op jit(solution)/shard_map/ppermute | solution.py:239
  219.2 43.8 %collective-permute-start.27 = (f32[1,64]{1,0:T(1,128)S(1)}, f32[1,64]{1,0:T(1,128)S(1)}, u32[]{:S(2)}, u32[]{:S(2)}) collective-permute-start(f32[1,64]{1,0:T(1,128)S(1)} %add.616), channel_id=1, source_target_pairs={{0,2},{2,0},{1,3},{3,1},{4,6},{6,4},{5,7},{7,5},{8,10},{10,8},{9,1... | collective-permute-start | bytes 776 | tf_op jit(solution)/shard_map/ppermute | solution.py:25
  260.1 5.5 %collective-permute-start.21 = (f32[512]{0:T(512)S(1)}, f32[512]{0:T(512)S(1)}, u32[]{:S(2)}, u32[]{:S(2)}) collective-permute-start(f32[512]{0:T(512)S(1)} %add.605), channel_id=1, source_target_pairs={{0,2},{2,0},{1,3},{3,1},{4,6},{6,4},{5,7},{7,5},{8,10},{10,8},{9,1... | collective-permute-start | bytes 6152 | tf_op jit(solution)/shard_map/ppermute | solution.py:25
  264.6 6.0 %collective-permute-start.23 = (f32[512,64]{0,1:T(8,128)S(1)}, f32[512,64]{0,1:T(8,128)S(1)}, u32[]{:S(2)}, u32[]{:S(2)}) collective-permute-start(f32[512,64]{0,1:T(8,128)S(1)} %add.612), channel_id=1, source_target_pairs={{0,2},{2,0},{1,3},{3,1},{4,6},{6,4},{5,7},{7,5},{8,10},{10,8},{9,1... | collective-permute-start | bytes 393224 | tf_op jit(solution)/shard_map/ppermute | solution.py:25
  (23 other events, 248.9 us)
where the time goes:
time: 282 us; the launch traced here: 276 us
  waiting for transfers between devices  130 us (46%)
  starting transfers between devices  66.9 us (24%)
  matrix products  34.8 us (12%)
  other arithmetic  24.9 us (9%)
  local copies, waits for them, and re-layouts  16.5 us (6%)
  between operations  3.35 us (1%)
    ppermute x11, waiting for transfers between devices, swapped(): return lax.ppermute(block, axis, route)  42.2 us
    ppermute x1, starting transfers between devices, on_device(): got_z = lax.ppermute(own, 'seq', to_other_z)  22.3 us
    ppermute x3, waiting for transfers between devices, on_device(): weight_parts.append(lax.ppermute(weight_send + hold, 'tp', route))  20.7 us
    ppermute x3, waiting for transfers between devices, on_device(): parts.append(lax.ppermute(hidden, 'tp', route))  19.2 us
    dot_general x8, matrix products, fold_block(): jnp.einsum('hqk,hkd->hqd', exps.astype(jnp.bfloat16), value_block, prefer...  16.3 us
    ppermute x2, waiting for transfers between devices, on_device(): z_from_right, far_keys = lax.ppermute((got_z, got_right[0]), 'seq', to_left)  15.4 us
    ppermute x3, waiting for transfers between devices, on_device(): attended_parts.append(lax.ppermute(attended, 'tp', route))  11.7 us
    ppermute x11, starting transfers between devices, swapped(): return lax.ppermute(block, axis, route)  11.3 us
  transfers between devices with their start and end apart: 29, of which 17 were waited for; matrix products, arithmetic and copies ran while one was open for 27% of the time, Pallas kernels for 0%

commit v1 on v0

--- a/solution.py
+++ b/solution.py
@@ -140,9 +140,14 @@
     local_width = hidden.shape[1]
     tp_count = lax.axis_size("tp")
     parts = [hidden]
+    weight_parts = [lax.dynamic_slice_in_dim(out_weight, tp_pos * local_width, local_width, 1)]
     for shift in range(1, tp_count):
         route = [(src, (src + shift) % tp_count) for src in range(tp_count)]
-        parts.append(lax.ppermute(hidden, "tp", route))
+        dest = (tp_pos + shift) % tp_count
+        weight_send = lax.dynamic_slice_in_dim(out_weight, dest * local_width, local_width, 1)
+        hidden_part, weight_part = lax.ppermute((hidden, weight_send), "tp", route)
+        parts.append(hidden_part)
+        weight_parts.append(weight_part)
     stacked = jnp.stack(parts)
     gathered = jnp.concatenate(
         [
@@ -228,14 +233,9 @@
     row_max, row_sum, weighted = softmax_state
     attended = (weighted / row_sum[:, :, None]).astype(jnp.bfloat16)
     log_sums = row_max + jnp.log(row_sum)
-    hold = jnp.minimum(jnp.abs(queries[0, 0, 0]), 0).astype(out_weight.dtype)
     attended_parts = [attended]
-    weight_parts = [lax.dynamic_slice_in_dim(out_weight, tp_pos * local_width, local_width, 1)]
     for shift in range(1, tp_count):
         route = [(src, (src + shift) % tp_count) for src in range(tp_count)]
-        dest = (tp_pos + shift) % tp_count
-        weight_send = lax.dynamic_slice_in_dim(out_weight, dest * local_width, local_width, 1)
-        weight_parts.append(lax.ppermute(weight_send + hold, "tp", route))
         attended_parts.append(lax.ppermute(attended, "tp", route))
     all_attended = jnp.stack(attended_parts)
     all_weights = jnp.stack(weight_parts).reshape(tp_count, heads_here, head_dim, local_width)

time: 282 us -> 320 us (1.13)
  waiting for transfers between devices: 130 us -> 181 us
  starting transfers between devices: 66.9 us -> 55.6 us
    ppermute x3, waiting for transfers between devices: 11.7 us -> 29.8 us  [on_device(): attended_parts.append(lax.ppermute(attended, 'tp', route))]
    ppermute x1, starting transfers between devices: 22.3 us -> 5.52 us  [on_device(): got_z = lax.ppermute(own, 'seq', to_other_z)]
    ppermute x11, waiting for transfers between devices: 42.2 us -> 55.3 us  [swapped(): return lax.ppermute(block, axis, route)]
    ppermute x11, starting transfers between devices: 11.3 us -> 20.5 us  [swapped(): return lax.ppermute(block, axis, route)]
    ppermute x1, waiting for transfers between devices: 5.46 us -> 13.6 us  [on_device(): got_right = lax.ppermute(own, 'seq', to_left)]
    ppermute x6, waiting for transfers between devices: 39.9 us -> 47.4 us  [on_device(): hidden_part, weight_part = lax.ppermute((hidden, weight_send), 'tp', route)]
    ppermute x1, waiting for transfers between devices: 0.01 us -> 5.14 us  [on_device(): got_left = lax.ppermute(own, 'seq', to_right)]
    ppermute x2, starting transfers between devices: 8.7 us -> 5.26 us  [on_device(): z_from_right, far_keys = lax.ppermute((got_z, got_right[0]), 'seq', to_left)]
  transfers between devices with their start and end apart: 29 -> 29, of which waited for: 17 -> 16; matrix products, arithmetic and copies ran while one was open for 27% -> 24% of each run, Pallas kernels for 0% -> 0%
where the time goes in v1:
time: 320 us; the launch traced here: 314 us
  waiting for transfers between devices  181 us (57%)
  starting transfers between devices  55.6 us (17%)
  matrix products  34.8 us (11%)
  other arithmetic  22.7 us (7%)
  local copies, waits for them, and re-layouts  17.5 us (5%)
    ppermute x11, waiting for transfers between devices, swapped(): return lax.ppermute(block, axis, route)  55.3 us
    ppermute x6, waiting for transfers between devices, on_device(): hidden_part, weight_part = lax.ppermute((hidden, weight_send), 'tp', route)  47.4 us
    ppermute x3, waiting for transfers between devices, on_device(): attended_parts.append(lax.ppermute(attended, 'tp', route))  29.8 us
    ppermute x11, starting transfers between devices, swapped(): return lax.ppermute(block, axis, route)  20.5 us
    dot_general x8, matrix products, fold_block(): jnp.einsum('hqk,hkd->hqd', exps.astype(jnp.bfloat16), value_block, prefer...  16.6 us
    ppermute x1, waiting for transfers between devices, on_device(): got_right = lax.ppermute(own, 'seq', to_left)  13.6 us
    ppermute x2, waiting for transfers between devices, on_device(): z_from_right, far_keys = lax.ppermute((got_z, got_right[0]), 'seq', to_left)  12.4 us
    unnamed x35, local copies, waits for them, and re-layouts  10.4 us
  transfers between devices with their start and end apart: 29, of which 16 were waited for; matrix products, arithmetic and copies ran while one was open for 24% of the time, Pallas kernels for 0%

profile of v1, /device:TPU:40, one launch (start us, length us, event | category | flops | bytes accessed | tf_op | source)
XLA Modules:
  0.0 314.1 jit_solution(13700166161514076002)
XLA Ops:
  6.0 3.1 constant_dynamic-slice_fusion.3
  12.8 10.3 %copy.27 = bf16[3072,3,384]{0,2,1:T(8,128)(2,1)} copy(bf16[3072,3,384]{2,0,1:T(8,128)(2,1)} %param.18) | data formatting | bytes 14155776 | tf_op args[6]
  29.4 43.6 %collective-permute-done.24 = f32[1,64]{1,0:T(1,128)S(1)} collective-permute-done((f32[1,64]{1,0:T(1,128)S(1)}, f32[1,64]{1,0:T(1,128)S(1)}, u32[]{:S(2)}, u32[]{:S(2)}) %collective-permute-start.24) | collective-permute-done | bytes 288 | tf_op jit(solution)/shard_map/ppermute | solution.py:25
  76.8 47.4 %collective-permute-done.1 = bf16[576,768]{1,0:T(8,128)(2,1)} collective-permute-done((bf16[576,768]{1,0:T(8,128)(2,1)}, bf16[576,768]{1,0:T(8,128)(2,1)}, u32[]{:S(2)}, u32[]{:S(2)}) %collective-permute-start.1) | collective-permute-done | bytes 884768 | tf_op jit(solution)/shard_map/ppermute | solution.py:148
  126.2 3.3 %convert_reduce_fusion = (f32[576]{0:T(1024)S(1)}, f32[576]{0:T(1024)S(1)}) fusion(bf16[576,768]{1,0:T(8,128)(2,1)S(1)} %get-tuple-element.32, bf16[576,768]{1,0:T(8,128)(2,1)S(1)} %get-tuple-element.33, bf16[576,768]{1,0:T(8,128)(2,1)S(1)} %get-tuple-element.34, bf16[576,768]{1,0:T(8,128)(2,1)S(1)} %get-tuple-element.31), kind=kLoop, calls=%fused_computation.2 | loop fusion | flops 19463040 | bytes 3543552 | tf_op jit(solution)/shard_map/reduce_sum | solution.py:62
  129.6 5.2 %fusion.71 = f32[3,3,576,128]{3,2,1,0:T(8,128)S(1)} fusion(bf16[3072,3,3,128]{0,3,2,1:T(8,128)(2,1)S(1)} %bitcast.140, f32[3072]{0:T(1024)S(1)} %bitcast.145, f32[3072]{0:T(1024)S(1)} %bitcast.144, f32[576]{0:T(1024)S(1)} %get-tuple-element.60, f32[576]{0:T(1024)S(1)} %get-tuple-element.59, bf16[576,768]{1,0:T(8,128)(2,1)S(1)} %get-tuple-element.32, ...), kind=kOutput, calls=%fused_computation.88 | convolution fusion | flops 4099866624 | bytes 13300224 | tf_op jit(solution)/shard_map/rf,fchd->chrd/dot_general | solution.py:170
  138.3 5.5 %collective-permute-start.3 = (bf16[2,3,576,128]{3,2,1,0:T(8,128)(2,1)S(1)}, bf16[2,3,576,128]{3,2,1,0:T(8,128)(2,1)S(1)}, u32[]{:S(2)}, u32[]{:S(2)}) collective-permute-start(bf16[2,3,576,128]{3,2,1,0:T(8,128)(2,1)S(1)} %pad_maximum_fusion.3), channel_id=1, source_target_pairs={{0,4},{4,0},{8,12},{12,8},{16,20},{20,16},{24,28},{28,24},{32,36},... | collective-permute-start | bytes 2654216 | tf_op jit(solution)/shard_map/ppermute | solution.py:186
  143.8 3.1 collective-permute-start.4
  150.0 13.6 %collective-permute-done.4 = bf16[2,3,576,128]{3,2,1,0:T(8,128)(2,1)S(1)} collective-permute-done((bf16[2,3,576,128]{3,2,1,0:T(8,128)(2,1)S(1)}, bf16[2,3,576,128]{3,2,1,0:T(8,128)(2,1)S(1)}, u32[]{:S(2)}, u32[]{:S(2)}) %collective-permute-start.4) | collective-permute-done | bytes 884768 | tf_op jit(solution)/shard_map/ppermute | solution.py:187
  165.7 9.3 %collective-permute-done.3 = bf16[2,3,576,128]{3,2,1,0:T(8,128)(2,1)S(1)} collective-permute-done((bf16[2,3,576,128]{3,2,1,0:T(8,128)(2,1)S(1)}, bf16[2,3,576,128]{3,2,1,0:T(8,128)(2,1)S(1)}, u32[]{:S(2)}, u32[]{:S(2)}) %collective-permute-start.3) | collective-permute-done | bytes 884768 | tf_op jit(solution)/shard_map/ppermute | solution.py:186
  174.9 2.8 collective-permute-start.10
  178.6 5.1 %collective-permute-done.5 = bf16[2,3,576,128]{3,2,1,0:T(8,128)(2,1)S(1)} collective-permute-done((bf16[2,3,576,128]{3,2,1,0:T(8,128)(2,1)S(1)}, bf16[2,3,576,128]{3,2,1,0:T(8,128)(2,1)S(1)}, u32[]{:S(2)}, u32[]{:S(2)}) %collective-permute-start.5) | collective-permute-done | bytes 884768 | tf_op jit(solution)/shard_map/ppermute | solution.py:188
  190.1 12.4 %collective-permute-done.6 = bf16[2,3,576,128]{3,2,1,0:T(8,128)(2,1)S(1)} collective-permute-done((bf16[2,3,576,128]{3,2,1,0:T(8,128)(2,1)S(1)}, bf16[2,3,576,128]{3,2,1,0:T(8,128)(2,1)S(1)}, u32[]{:S(2)}, u32[]{:S(2)}) %collective-permute-start.6) | collective-permute-done | bytes 884768 | tf_op jit(solution)/shard_map/ppermute | solution.py:197
  204.6 2.8 collective-permute-start.7
  208.2 5.1 %collective-permute-done.7 = bf16[3,576,128]{2,1,0:T(8,128)(2,1)S(1)} collective-permute-done((bf16[3,576,128]{2,1,0:T(8,128)(2,1)S(1)}, bf16[3,576,128]{2,1,0:T(8,128)(2,1)S(1)}, u32[]{:S(2)}, u32[]{:S(2)}) %collective-permute-start.7) | collective-permute-done | bytes 442400 | tf_op jit(solution)/shard_map/ppermute | solution.py:211
  231.3 2.8 fusion.119
  235.9 11.4 %collective-permute-start.25 = (f32[1,64]{1,0:T(1,128)S(1)}, f32[1,64]{1,0:T(1,128)S(1)}, u32[]{:S(2)}, u32[]{:S(2)}) collective-permute-start(f32[1,64]{1,0:T(1,128)S(1)} %add.596), channel_id=1, source_target_pairs={{0,2},{2,0},{1,3},{3,1},{4,6},{6,4},{5,7},{7,5},{8,10},{10,8},{9,1... | collective-permute-start | bytes 776 | tf_op jit(solution)/shard_map/ppermute | solution.py:25
  253.6 3.8 %collective-permute-start.13 = (bf16[3,576,128]{2,1,0:T(8,128)(2,1)S(1)}, bf16[3,576,128]{2,1,0:T(8,128)(2,1)S(1)}, u32[]{:S(2)}, u32[]{:S(2)}) collective-permute-start(bf16[3,576,128]{2,1,0:T(8,128)(2,1)S(1)} %fusion.134), channel_id=1, source_target_pairs={{0,2},{1,3},{2,0},{3,1},{4,6},{5,7},{6,4},{7,5},{8,10},{9,11},{10,... | collective-permute-start | bytes 1327112 | tf_op jit(solution)/shard_map/ppermute | solution.py:239
  260.3 21.5 %collective-permute-done.12 = bf16[3,576,128]{2,1,0:T(8,128)(2,1)S(1)} collective-permute-done((bf16[3,576,128]{2,1,0:T(8,128)(2,1)S(1)}, bf16[3,576,128]{2,1,0:T(8,128)(2,1)S(1)}, u32[]{:S(2)}, u32[]{:S(2)}) %collective-permute-start.12) | collective-permute-done | bytes 442400 | tf_op jit(solution)/shard_map/ppermute | solution.py:239
  281.7 4.7 %collective-permute-done.13 = bf16[3,576,128]{2,1,0:T(8,128)(2,1)S(1)} collective-permute-done((bf16[3,576,128]{2,1,0:T(8,128)(2,1)S(1)}, bf16[3,576,128]{2,1,0:T(8,128)(2,1)S(1)}, u32[]{:S(2)}, u32[]{:S(2)}) %collective-permute-start.13) | collective-permute-done | bytes 442400 | tf_op jit(solution)/shard_map/ppermute | solution.py:239
  286.5 3.6 %collective-permute-done.14 = bf16[3,576,128]{2,1,0:T(8,128)(2,1)} collective-permute-done((bf16[3,576,128]{2,1,0:T(8,128)(2,1)S(1)}, bf16[3,576,128]{2,1,0:T(8,128)(2,1)}, u32[]{:S(2)}, u32[]{:S(2)}) %collective-permute-start.14) | collective-permute-done | bytes 442400 | tf_op jit(solution)/shard_map/ppermute | solution.py:239
  290.1 3.1 fusion.69
  302.7 5.8 %collective-permute-done.23 = f32[512,64]{0,1:T(8,128)S(1)} collective-permute-done((f32[512,64]{0,1:T(8,128)S(1)}, f32[512,64]{0,1:T(8,128)S(1)}, u32[]{:S(2)}, u32[]{:S(2)}) %collective-permute-start.23) | collective-permute-done | bytes 131104 | tf_op jit(solution)/shard_map/ppermute | solution.py:25
  310.0 3.0 collective-permute-done.28
  (155 shorter events, 79.0 us)
Async XLA Ops:
  0.7 73.6 %collective-permute-start = (bf16[576,768]{1,0:T(8,128)(2,1)}, bf16[576,768]{1,0:T(8,128)(2,1)S(1)}, u32[]{:S(2)}, u32[]{:S(2)}) collective-permute-start(bf16[576,768]{1,0:T(8,128)(2,1)} %param.12), channel_id=1, source_target_pairs={{0,1},{1,2},{2,3},{3,0},{4,5},{5,6},{6,7},{7,4},{8,9},{9,10},{10,1... | collective-permute-start | bytes 2654216 | tf_op jit(solution)/shard_map/ppermute | solution.py:148
  2.7 121.5 %collective-permute-start.1 = (bf16[576,768]{1,0:T(8,128)(2,1)}, bf16[576,768]{1,0:T(8,128)(2,1)}, u32[]{:S(2)}, u32[]{:S(2)}) collective-permute-start(bf16[576,768]{1,0:T(8,128)(2,1)} %param.12), channel_id=1, source_target_pairs={{0,2},{1,3},{2,0},{3,1},{4,6},{5,7},{6,4},{7,5},{8,10},{9,11},{10,... | collective-permute-start | bytes 2654216 | tf_op jit(solution)/shard_map/ppermute | solution.py:148
  4.1 120.0 %collective-permute-start.2 = (bf16[576,768]{1,0:T(8,128)(2,1)}, bf16[576,768]{1,0:T(8,128)(2,1)}, u32[]{:S(2)}, u32[]{:S(2)}) collective-permute-start(bf16[576,768]{1,0:T(8,128)(2,1)} %param.12), channel_id=1, source_target_pairs={{0,3},{1,0},{2,1},{3,2},{4,7},{5,4},{6,5},{7,6},{8,11},{9,8},{10,9... | collective-permute-start | bytes 2654216 | tf_op jit(solution)/shard_map/ppermute | solution.py:148
  9.1 248.3 %collective-permute-start.15 = (bf16[384,768]{1,0:T(8,128)(2,1)}, bf16[384,768]{1,0:T(8,128)(2,1)}, u32[]{:S(2)}, u32[]{:S(2)}) collective-permute-start(bf16[384,768]{1,0:T(8,128)(2,1)} %get-tuple-element.38), channel_id=1, source_target_pairs={{0,1},{1,2},{2,3},{3,0},{4,5},{5,6},{6,7},{7,4},{8,9},{9,10},{10,1... | collective-permute-start | bytes 1769480 | tf_op jit(solution)/shard_map/ppermute | solution.py:148
  10.1 62.9 %collective-permute-start.24 = (f32[1,64]{1,0:T(1,128)S(1)}, f32[1,64]{1,0:T(1,128)S(1)}, u32[]{:S(2)}, u32[]{:S(2)}) collective-permute-start(f32[1,64]{1,0:T(1,128)S(1)} %fusion.170), channel_id=1, source_target_pairs={{0,1},{1,0},{2,3},{3,2},{4,5},{5,4},{6,7},{7,6},{8,9},{9,8},{10,11... | collective-permute-start | bytes 776 | tf_op jit(solution)/shard_map/ppermute | solution.py:25
  73.0 186.0 %collective-permute-start.16 = (bf16[384,768]{1,0:T(8,128)(2,1)}, bf16[384,768]{1,0:T(8,128)(2,1)}, u32[]{:S(2)}, u32[]{:S(2)}) collective-permute-start(bf16[384,768]{1,0:T(8,128)(2,1)} %get-tuple-element.40), channel_id=1, source_target_pairs={{0,2},{1,3},{2,0},{3,1},{4,6},{5,7},{6,4},{7,5},{8,10},{9,11},{10,... | collective-permute-start | bytes 1769480 | tf_op jit(solution)/shard_map/ppermute | solution.py:148
  74.2 186.0 %collective-permute-start.17 = (bf16[384,768]{1,0:T(8,128)(2,1)}, bf16[384,768]{1,0:T(8,128)(2,1)}, u32[]{:S(2)}, u32[]{:S(2)}) collective-permute-start(bf16[384,768]{1,0:T(8,128)(2,1)} %get-tuple-element.39), channel_id=1, source_target_pairs={{0,3},{1,0},{2,1},{3,2},{4,7},{5,4},{6,5},{7,6},{8,11},{9,8},{10,9... | collective-permute-start | bytes 1769480 | tf_op jit(solution)/shard_map/ppermute | solution.py:148
  138.3 36.6 %collective-permute-start.3 = (bf16[2,3,576,128]{3,2,1,0:T(8,128)(2,1)S(1)}, bf16[2,3,576,128]{3,2,1,0:T(8,128)(2,1)S(1)}, u32[]{:S(2)}, u32[]{:S(2)}) collective-permute-start(bf16[2,3,576,128]{3,2,1,0:T(8,128)(2,1)S(1)} %pad_maximum_fusion.3), channel_id=1, source_target_pairs={{0,4},{4,0},{8,12},{12,8},{16,20},{20,16},{24,28},{28,24},{32,36},... | collective-permute-start | bytes 2654216 | tf_op jit(solution)/shard_map/ppermute | solution.py:186
  143.8 19.8 %collective-permute-start.4 = (bf16[2,3,576,128]{3,2,1,0:T(8,128)(2,1)S(1)}, bf16[2,3,576,128]{3,2,1,0:T(8,128)(2,1)S(1)}, u32[]{:S(2)}, u32[]{:S(2)}) collective-permute-start(bf16[2,3,576,128]{3,2,1,0:T(8,128)(2,1)S(1)} %pad_maximum_fusion.3), channel_id=1, source_target_pairs={{0,24},{4,28},{8,0},{12,4},{16,8},{20,12},{24,16},{28,20},{32,56},... | collective-permute-start | bytes 2654216 | tf_op jit(solution)/shard_map/ppermute | solution.py:187
  163.6 20.1 %collective-permute-start.5 = (bf16[2,3,576,128]{3,2,1,0:T(8,128)(2,1)S(1)}, bf16[2,3,576,128]{3,2,1,0:T(8,128)(2,1)S(1)}, u32[]{:S(2)}, u32[]{:S(2)}) collective-permute-start(bf16[2,3,576,128]{3,2,1,0:T(8,128)(2,1)S(1)} %pad_maximum_fusion.3), channel_id=1, source_target_pairs={{0,8},{4,12},{8,16},{12,20},{16,24},{20,28},{24,0},{28,4},{32,40},... | collective-permute-start | bytes 2654216 | tf_op jit(solution)/shard_map/ppermute | solution.py:188
  174.9 12.1 %collective-permute-start.10 = (bf16[3,576,128]{2,1,0:T(8,128)(2,1)S(1)}, bf16[3,576,128]{2,1,0:T(8,128)(2,1)S(1)}, u32[]{:S(2)}, u32[]{:S(2)}) collective-permute-start(bf16[3,576,128]{2,1,0:T(8,128)(2,1)S(1)} %slice_bitcast_fusion.12), channel_id=1, source_target_pairs={{0,24},{4,28},{8,0},{12,4},{16,8},{20,12},{24,16},{28,20},{32,56},... | collective-permute-start | bytes 1327112 | tf_op jit(solution)/shard_map/ppermute | solution.py:197
  183.7 18.8 %collective-permute-start.6 = (bf16[2,3,576,128]{3,2,1,0:T(8,128)(2,1)S(1)}, bf16[2,3,576,128]{3,2,1,0:T(8,128)(2,1)S(1)}, u32[]{:S(2)}, u32[]{:S(2)}) collective-permute-start(bf16[2,3,576,128]{3,2,1,0:T(8,128)(2,1)S(1)} %collective-permute-done.3), channel_id=1, source_target_pairs={{0,24},{4,28},{8,0},{12,4},{16,8},{20,12},{24,16},{28,20},{32,56},... | collective-permute-start | bytes 2654216 | tf_op jit(solution)/shard_map/ppermute | solution.py:197
  187.0 17.6 %collective-permute-start.8 = (bf16[2,3,576,128]{3,2,1,0:T(8,128)(2,1)S(1)}, bf16[2,3,576,128]{3,2,1,0:T(8,128)(2,1)S(1)}, u32[]{:S(2)}, u32[]{:S(2)}) collective-permute-start(bf16[2,3,576,128]{3,2,1,0:T(8,128)(2,1)S(1)} %collective-permute-done.3), channel_id=1, source_target_pairs={{0,8},{4,12},{8,16},{12,20},{16,24},{20,28},{24,0},{28,4},{32,40},... | collective-permute-start | bytes 2654216 | tf_op jit(solution)/shard_map/ppermute | solution.py:198
  202.5 50.7 %collective-permute-start.26 = (f32[1,64]{1,0:T(1,128)S(1)}, f32[1,64]{1,0:T(1,128)S(1)}, u32[]{:S(2)}, u32[]{:S(2)}) collective-permute-start(f32[1,64]{1,0:T(1,128)S(1)} %fusion.169), channel_id=1, source_target_pairs={{0,1},{1,0},{2,3},{3,2},{4,5},{5,4},{6,7},{7,6},{8,9},{9,8},{10,11... | collective-permute-start | bytes 776 | tf_op jit(solution)/shard_map/ppermute | solution.py:25
  204.6 8.8 %collective-permute-start.7 = (bf16[3,576,128]{2,1,0:T(8,128)(2,1)S(1)}, bf16[3,576,128]{2,1,0:T(8,128)(2,1)S(1)}, u32[]{:S(2)}, u32[]{:S(2)}) collective-permute-start(bf16[3,576,128]{2,1,0:T(8,128)(2,1)S(1)} %slice_bitcast_fusion.6), channel_id=1, source_target_pairs={{0,24},{4,28},{8,0},{12,4},{16,8},{20,12},{24,16},{28,20},{32,56},... | collective-permute-start | bytes 1327112 | tf_op jit(solution)/shard_map/ppermute | solution.py:211
  213.3 12.8 %collective-permute-start.9 = (bf16[3,576,128]{2,1,0:T(8,128)(2,1)S(1)}, bf16[3,576,128]{2,1,0:T(8,128)(2,1)}, u32[]{:S(2)}, u32[]{:S(2)}) collective-permute-start(bf16[3,576,128]{2,1,0:T(8,128)(2,1)S(1)} %slice_bitcast_fusion.5), channel_id=1, source_target_pairs={{0,8},{4,12},{8,16},{12,20},{16,24},{20,28},{24,0},{28,4},{32,40},... | collective-permute-start | bytes 1327112 | tf_op jit(solution)/shard_map/ppermute | solution.py:212
  226.1 9.8 %collective-permute-start.11 = (bf16[3,576,128]{2,1,0:T(8,128)(2,1)S(1)}, bf16[3,576,128]{2,1,0:T(8,128)(2,1)S(1)}, u32[]{:S(2)}, u32[]{:S(2)}) collective-permute-start(bf16[3,576,128]{2,1,0:T(8,128)(2,1)S(1)} %slice_bitcast_fusion.7), channel_id=1, source_target_pairs={{0,8},{4,12},{8,16},{12,20},{16,24},{20,28},{24,0},{28,4},{32,40},... | collective-permute-start | bytes 1327112 | tf_op jit(solution)/shard_map/ppermute | solution.py:198
  235.9 17.6 %collective-permute-start.25 = (f32[1,64]{1,0:T(1,128)S(1)}, f32[1,64]{1,0:T(1,128)S(1)}, u32[]{:S(2)}, u32[]{:S(2)}) collective-permute-start(f32[1,64]{1,0:T(1,128)S(1)} %add.596), channel_id=1, source_target_pairs={{0,2},{2,0},{1,3},{3,1},{4,6},{6,4},{5,7},{7,5},{8,10},{10,8},{9,1... | collective-permute-start | bytes 776 | tf_op jit(solution)/shard_map/ppermute | solution.py:25
  253.3 28.5 %collective-permute-start.12 = (bf16[3,576,128]{2,1,0:T(8,128)(2,1)S(1)}, bf16[3,576,128]{2,1,0:T(8,128)(2,1)S(1)}, u32[]{:S(2)}, u32[]{:S(2)}) collective-permute-start(bf16[3,576,128]{2,1,0:T(8,128)(2,1)S(1)} %fusion.134), channel_id=1, source_target_pairs={{0,1},{1,2},{2,3},{3,0},{4,5},{5,6},{6,7},{7,4},{8,9},{9,10},{10,1... | collective-permute-start | bytes 1327112 | tf_op jit(solution)/shard_map/ppermute | solution.py:239
  253.6 32.9 %collective-permute-start.13 = (bf16[3,576,128]{2,1,0:T(8,128)(2,1)S(1)}, bf16[3,576,128]{2,1,0:T(8,128)(2,1)S(1)}, u32[]{:S(2)}, u32[]{:S(2)}) collective-permute-start(bf16[3,576,128]{2,1,0:T(8,128)(2,1)S(1)} %fusion.134), channel_id=1, source_target_pairs={{0,2},{1,3},{2,0},{3,1},{4,6},{5,7},{6,4},{7,5},{8,10},{9,11},{10,... | collective-permute-start | bytes 1327112 | tf_op jit(solution)/shard_map/ppermute | solution.py:239
  257.4 32.6 %collective-permute-start.14 = (bf16[3,576,128]{2,1,0:T(8,128)(2,1)S(1)}, bf16[3,576,128]{2,1,0:T(8,128)(2,1)}, u32[]{:S(2)}, u32[]{:S(2)}) collective-permute-start(bf16[3,576,128]{2,1,0:T(8,128)(2,1)S(1)} %fusion.134), channel_id=1, source_target_pairs={{0,3},{1,0},{2,1},{3,2},{4,7},{5,4},{6,5},{7,6},{8,11},{9,8},{10,9... | collective-permute-start | bytes 1327112 | tf_op jit(solution)/shard_map/ppermute | solution.py:239
  259.0 41.1 %collective-permute-start.27 = (f32[1,64]{1,0:T(1,128)S(1)}, f32[1,64]{1,0:T(1,128)S(1)}, u32[]{:S(2)}, u32[]{:S(2)}) collective-permute-start(f32[1,64]{1,0:T(1,128)S(1)} %add.598), channel_id=1, source_target_pairs={{0,2},{2,0},{1,3},{3,1},{4,6},{6,4},{5,7},{7,5},{8,10},{10,8},{9,1... | collective-permute-start | bytes 776 | tf_op jit(solution)/shard_map/ppermute | solution.py:25
  296.6 5.9 %collective-permute-start.22 = (f32[512,64]{0,1:T(8,128)S(1)}, f32[512,64]{0,1:T(8,128)S(1)}, u32[]{:S(2)}, u32[]{:S(2)}) collective-permute-start(f32[512,64]{0,1:T(8,128)S(1)} %fusion.75), channel_id=1, source_target_pairs={{0,1},{1,0},{2,3},{3,2},{4,5},{5,4},{6,7},{7,6},{8,9},{9,8},{10,11... | collective-permute-start | bytes 393224 | tf_op jit(solution)/shard_map/ppermute | solution.py:25
  302.6 6.0 %collective-permute-start.23 = (f32[512,64]{0,1:T(8,128)S(1)}, f32[512,64]{0,1:T(8,128)S(1)}, u32[]{:S(2)}, u32[]{:S(2)}) collective-permute-start(f32[512,64]{0,1:T(8,128)S(1)} %add.594), channel_id=1, source_target_pairs={{0,2},{2,0},{1,3},{3,1},{4,6},{6,4},{5,7},{7,5},{8,10},{10,8},{9,1... | collective-permute-start | bytes 393224 | tf_op jit(solution)/shard_map/ppermute | solution.py:25
  (22 other events, 305.5 us)
